TPU v7x, 32 devices: a whole 2x2x4 slice. The times are simulated.
32 devices in a mesh: grp: 2 (over x), chan: 16 (over z, y, core).
Axes of the slice: x: 2, y: 2, z: 4, core: 2. Of those that a mesh axis runs over, the one named last changes fastest.
Arguments:
- samples: bfloat16 [128, 62, 8192], P('chan', 'grp'), parts along dimension 1, may hold values from -6 to 6
- eq_gain: float32 [128, 4096], P('chan'), may hold values from 0.5 to 2
- delays: float32 [1024, 64], replicated, may hold values from -64 to 64
Outputs:
- beams: bfloat16 [2, 1024, 4096], P('grp', 'chan'), parts along dimension 0
There are 2 independent parts, one for each index of `grp`. A program takes and returns all parts, laid end to end along the dimension named above; an argument that names none is the same for every part. Nothing has to cross between parts.
All inputs are finite; a program needn't handle non-finite values.
Results may differ from a plain program's by a relative error of at most 0.0034.
Values may be sent and summed in bfloat16 or wider, within the bound.
No kernel may reach another device: no remote copies, remote signals or barrier semaphores. Data moves between devices by JAX's collectives and lax.ppermute only.
A program may use at most 448 MiB of HBM per device.

v0:
```python
import math
import jax
import jax.numpy as jnp
from jax import lax
from jax.sharding import PartitionSpec as P

DISHES = 64
POLS = 2
NB = 1024
TAPS = 16
AVG = 16
SPEC = 16


def pfb_taps(frame_len, tap_count):
    tap_total = tap_count * frame_len
    position = jnp.arange(tap_total, dtype=jnp.float32) + 0.5
    window = 0.5 - 0.5 * jnp.cos(2.0 * math.pi / tap_total * position)
    offset = (position - 0.5 * tap_total) / frame_len
    prototype = window * jnp.sin(math.pi * offset) / (math.pi * offset)
    prototype = prototype / jnp.sqrt(jnp.sum(prototype * prototype))
    return prototype.reshape(tap_count, frame_len)


def cos_sin(numer, denom):
    phase_angle = 2.0 * math.pi / denom * numer.astype(jnp.float32)
    return (jnp.cos(phase_angle), -jnp.sin(phase_angle))


def turn_tables(frame_len):
    outer_len = 2 ** ((frame_len.bit_length() - 1) // 2)
    inner_len = frame_len // outer_len
    half_len = inner_len // 2
    outer_index = jnp.arange(outer_len, dtype=jnp.int32)
    inner_index = jnp.arange(inner_len, dtype=jnp.int32)
    half_index = jnp.arange(half_len, dtype=jnp.int32)
    one_cos, one_sin = cos_sin(outer_index[:, None] * outer_index[None, :] % outer_len, outer_len)
    twist_cos, twist_sin = cos_sin(
        outer_index[:, None] * inner_index[None, :] % frame_len, frame_len
    )
    three_cos, three_sin = cos_sin(
        inner_index[:, None] * half_index[None, :] % inner_len, inner_len
    )
    table_one = jnp.stack([one_cos, one_sin])
    table_three = jnp.stack([three_cos, three_sin])
    return (outer_len, inner_len, table_one, twist_cos, twist_sin, table_three)


def body(samples, eq_gain, delays):
    inputs_here, frame_count, frame_len = samples.shape
    chan_count = frame_len // 2
    groups = lax.axis_size("chan")
    my_index = lax.axis_index("chan")
    chan_here = chan_count // groups
    beams_here = NB // groups
    time_bins = SPEC // AVG
    highest = lax.Precision.HIGHEST
    tap_table = pfb_taps(frame_len, TAPS)
    filtered = jnp.zeros((inputs_here, SPEC, frame_len), jnp.float32)
    for tap_index in range(TAPS):
        filtered = filtered + tap_table[tap_index] * samples[
            :, tap_index : tap_index + SPEC, :
        ].astype(jnp.float32)
    outer_len, inner_len, table_one, twist_cos, twist_sin, table_three = turn_tables(frame_len)
    framed = filtered.reshape(inputs_here, SPEC, outer_len, inner_len)
    section_one = jnp.einsum("rkn,isnm->irskm", table_one, framed, precision=highest)
    real_one = section_one[:, 0]
    imag_one = section_one[:, 1]
    twisted = jnp.stack(
        [real_one * twist_cos - imag_one * twist_sin, real_one * twist_sin + imag_one * twist_cos],
        axis=1,
    )
    section_three = jnp.einsum("irskm,qmj->irqsjk", twisted, table_three, precision=highest)
    spec_real = (section_three[:, 0, 0] - section_three[:, 1, 1]).reshape(
        inputs_here, SPEC, chan_count
    )
    spec_imag = (section_three[:, 0, 1] + section_three[:, 1, 0]).reshape(
        inputs_here, SPEC, chan_count
    )
    gain_row = eq_gain[:, None, :]
    volt_real = (spec_real * gain_row).astype(jnp.bfloat16)
    volt_imag = (spec_imag * gain_row).astype(jnp.bfloat16)
    outgoing = jnp.stack([volt_real, volt_imag], axis=1).transpose(3, 1, 2, 0)
    arrived = lax.all_to_all(outgoing, "chan", split_axis=0, concat_axis=3, tiled=True)
    dish_volts = arrived.reshape(chan_here, 2, SPEC, DISHES, POLS).transpose(0, 1, 4, 2, 3)
    real_part = dish_volts[:, 0]
    imag_part = dish_volts[:, 1]
    volt_operand = jnp.stack(
        [
            jnp.concatenate([real_part, -imag_part], axis=-1),
            jnp.concatenate([imag_part, real_part], axis=-1),
        ],
        axis=1,
    ).reshape(chan_here, 2 * POLS * SPEC, 2 * DISHES)
    low_len = math.gcd(chan_here, 2 ** ((chan_here.bit_length() - 1) // 2))
    high_count = chan_here // low_len
    weight_scale = 1.0 / math.sqrt(DISHES)

    def rotation(channel, scale):
        turns = channel.astype(jnp.float32)[:, None, None] * delays[None, :, :] / frame_len
        turns = turns - jnp.round(turns)
        angle = 2.0 * math.pi * turns
        return (jnp.cos(angle) * scale, -jnp.sin(angle) * scale)

    high_channel = my_index * chan_here + jnp.arange(high_count, dtype=jnp.int32) * low_len
    high_real, high_imag = rotation(high_channel, weight_scale)
    low_real, low_imag = rotation(jnp.arange(low_len, dtype=jnp.int32), 1.0)
    volt_blocks = volt_operand.reshape(high_count, low_len, 2 * POLS * SPEC, 2 * DISHES)

    def one_block(block_args):
        base_real, base_imag, volt_part = block_args
        w_real = (base_real * low_real - base_imag * low_imag).astype(jnp.bfloat16)
        w_imag = (base_real * low_imag + base_imag * low_real).astype(jnp.bfloat16)
        weight_part = jnp.concatenate([w_real, w_imag], axis=-1)
        product = jnp.einsum(
            "cnk,cbk->cnb", volt_part, weight_part, preferred_element_type=jnp.float32
        ).reshape(low_len, 2 * POLS, time_bins, AVG, NB)
        return jnp.sum(product * product, axis=(1, 3)) / AVG

    energy = lax.map(one_block, (high_real, high_imag, volt_blocks))
    power_bins = energy.reshape(chan_here, time_bins, NB).transpose(1, 2, 0).astype(jnp.bfloat16)
    return lax.all_to_all(power_bins, "chan", split_axis=1, concat_axis=2, tiled=True)


def solution(mesh):
    in_specs = (P("chan", "grp", None), P("chan", None), P())
    out_specs = P("grp", "chan", None)
    return jax.shard_map(body, mesh=mesh, in_specs=in_specs, out_specs=out_specs, check_vma=False)
```

profile of v0, /device:TPU:0, one launch (start us, length us, event | category | flops | bytes accessed | tf_op | source)
XLA Modules:
  0.0 574.8 jit_solution(7906501570208651804)
XLA Ops:
  9.0 16.8 %add_bitcast_fusion = f32[8,16,64,128,1]{3,0,2,1,4:T(8,128)S(1)} fusion(bf16[8,31,8192]{2,0,1:T(8,128)(2,1)} %param.5, f32[8192]{0:T(1024)S(1)} %get-tuple-element.151, f32[8192]{0:T(1024)S(1)} %get-tuple-element.152, f32[8192]{0:T(1024)S(1)} %get-tuple-element.153, f32[8192]{0:T(1024)S(1)} %get-tuple-element.154, f32[8192]{0:T(1024)S(1)} %get-tuple-element.155, ...), kind=kLoop, calls=%fused_computation.42 | loop fusion | flops 49283072 | bytes 38273024 | tf_op jit(solution)/shard_map/reshape | solution.py:65
  35.1 27.7 %fusion.27 = f32[8,2,2,16,64,64]{5,4,3,1,0,2:T(8,128)} fusion(f32[1,128,64]{1,2,0:T(8,128)S(1)} %get-tuple-element.174, f32[1,128,64]{1,2,0:T(8,128)S(1)} %get-tuple-element.175, f32[8,1,16,64,128]{4,3,1,2,0:T(8,128)S(1)} %get-tuple-element.145, f32[8,1,16,64,128]{4,3,1,2,0:T(8,128)S(1)} %get-tuple-element.144), kind=kOutput, calls=%fused_computation.30 | convolution fusion | flops 3223339008 | bytes 16842752 | tf_op jit(solution)/shard_map/irskm,qmj->irqsjk/dot_general | solution.py:73
  113.9 20.8 %reshape.329 = bf16[16,2,32768]{2,1,0:T(2,128)(2,1)} reshape(bf16[4096,2,8,16]{3,2,1,0:T(8,128)(2,1)} %bitcast_bitcast_fusion) | data formatting | bytes 4194304
  142.4 17.0 %negate_multiply_fusion = (f32[16,1024,64]{1,2,0:T(8,128)}, f32[16,1024,64]{1,2,0:T(8,128)}) fusion(f32[1024,64]{0,1:T(8,128)S(1)} %copy-done, f32[16]{0:T(128)S(1)} %add_convert_fusion), kind=kLoop, calls=%fused_computation.38 | loop fusion | flops 8388608 | bytes 8650816 | tf_op jit(solution)/shard_map/mul | solution.py:103
  159.4 24.0 %all-to-all-done = bf16[16,2,32768]{2,1,0:T(2,128)(2,1)S(1)} async-done(((bf16[16,2,32768]{2,1,0:T(2,128)(2,1)}), bf16[16,2,32768]{2,1,0:T(2,128)(2,1)S(1)}, u32[]{:S(2)}, u32[]{:S(2)}) %all-to-all-start) | async-done | bytes 2097184 | tf_op jit(solution)/shard_map/all_to_all | solution.py:84
  197.8 14.6 %copy.59 = bf16[256,2,16,16,8]{0,2,4,3,1:T(8,128)(2,1)S(1)} copy(bf16[256,2,16,16,8]{2,4,1,0,3:T(8,128)(2,1)} %bitcast.87) | data formatting | bytes 4194304 | tf_op jit(solution)/shard_map/all_to_all | solution.py:84
  224.3 317.5 %while.12 = (s32[]{:T(128)}, bf16[16,16,1,1024]{3,1,0,2:T(8,128)(2,1)S(1)}, bf16[16,16,64,128]{3,2,1,0:T(8,128)(2,1)}, f32[16,1024,64]{1,2,0:T(8,128)}, f32[16,1...) while((s32[]{:T(128)}, ...), condition=%wide.region_3.4_spmd.clone.clone, body=%wide.region_1.3_spmd.clone.clone.sunk | while | flops 293601280 | bytes 10683037 | solution.py:120
  225.4 17.0 %fusion.84 = (bf16[16,1024,64]{1,2,0:T(8,128)(2,1)S(1)}, bf16[16,1024,64]{1,2,0:T(8,128)(2,1)S(1)}) fusion(f32[1024,64]{0,1:T(8,128)S(1)} %get-tuple-element.248, f32[16]{0:T(128)S(1)} %get-tuple-element.249, f32[1024,64]{0,1:T(8,128)S(1)} %get-tuple-element.223, f32[1024,64]{0,1:T(8,128)S(1)} %get-tuple-element.224), kind=kLoop, calls=%fused_computation.15.clone.1 | loop fusion | flops 14680064 | bytes 4980800 | tf_op jit(solution)/shard_map/while/body/eval_jaxpr/convert_element_type | solution.py:112
  245.2 17.0 %fusion.84 = (bf16[16,1024,64]{1,2,0:T(8,128)(2,1)S(1)}, bf16[16,1024,64]{1,2,0:T(8,128)(2,1)S(1)}) fusion(f32[1024,64]{0,1:T(8,128)S(1)} %get-tuple-element.248, f32[16]{0:T(128)S(1)} %get-tuple-element.249, f32[1024,64]{0,1:T(8,128)S(1)} %get-tuple-element.223, f32[1024,64]{0,1:T(8,128)S(1)} %get-tuple-element.224), kind=kLoop, calls=%fused_computation.15.clone.1 | loop fusion | flops 14680064 | bytes 4980800 | tf_op jit(solution)/shard_map/while/body/eval_jaxpr/convert_element_type | solution.py:112
  265.1 17.0 %fusion.84 = (bf16[16,1024,64]{1,2,0:T(8,128)(2,1)S(1)}, bf16[16,1024,64]{1,2,0:T(8,128)(2,1)S(1)}) fusion(f32[1024,64]{0,1:T(8,128)S(1)} %get-tuple-element.248, f32[16]{0:T(128)S(1)} %get-tuple-element.249, f32[1024,64]{0,1:T(8,128)S(1)} %get-tuple-element.223, f32[1024,64]{0,1:T(8,128)S(1)} %get-tuple-element.224), kind=kLoop, calls=%fused_computation.15.clone.1 | loop fusion | flops 14680064 | bytes 4980800 | tf_op jit(solution)/shard_map/while/body/eval_jaxpr/convert_element_type | solution.py:112
  284.9 17.0 %fusion.84 = (bf16[16,1024,64]{1,2,0:T(8,128)(2,1)S(1)}, bf16[16,1024,64]{1,2,0:T(8,128)(2,1)S(1)}) fusion(f32[1024,64]{0,1:T(8,128)S(1)} %get-tuple-element.248, f32[16]{0:T(128)S(1)} %get-tuple-element.249, f32[1024,64]{0,1:T(8,128)S(1)} %get-tuple-element.223, f32[1024,64]{0,1:T(8,128)S(1)} %get-tuple-element.224), kind=kLoop, calls=%fused_computation.15.clone.1 | loop fusion | flops 14680064 | bytes 4980800 | tf_op jit(solution)/shard_map/while/body/eval_jaxpr/convert_element_type | solution.py:112
  304.8 17.0 %fusion.84 = (bf16[16,1024,64]{1,2,0:T(8,128)(2,1)S(1)}, bf16[16,1024,64]{1,2,0:T(8,128)(2,1)S(1)}) fusion(f32[1024,64]{0,1:T(8,128)S(1)} %get-tuple-element.248, f32[16]{0:T(128)S(1)} %get-tuple-element.249, f32[1024,64]{0,1:T(8,128)S(1)} %get-tuple-element.223, f32[1024,64]{0,1:T(8,128)S(1)} %get-tuple-element.224), kind=kLoop, calls=%fused_computation.15.clone.1 | loop fusion | flops 14680064 | bytes 4980800 | tf_op jit(solution)/shard_map/while/body/eval_jaxpr/convert_element_type | solution.py:112
  324.6 17.0 %fusion.84 = (bf16[16,1024,64]{1,2,0:T(8,128)(2,1)S(1)}, bf16[16,1024,64]{1,2,0:T(8,128)(2,1)S(1)}) fusion(f32[1024,64]{0,1:T(8,128)S(1)} %get-tuple-element.248, f32[16]{0:T(128)S(1)} %get-tuple-element.249, f32[1024,64]{0,1:T(8,128)S(1)} %get-tuple-element.223, f32[1024,64]{0,1:T(8,128)S(1)} %get-tuple-element.224), kind=kLoop, calls=%fused_computation.15.clone.1 | loop fusion | flops 14680064 | bytes 4980800 | tf_op jit(solution)/shard_map/while/body/eval_jaxpr/convert_element_type | solution.py:112
  344.5 17.0 %fusion.84 = (bf16[16,1024,64]{1,2,0:T(8,128)(2,1)S(1)}, bf16[16,1024,64]{1,2,0:T(8,128)(2,1)S(1)}) fusion(f32[1024,64]{0,1:T(8,128)S(1)} %get-tuple-element.248, f32[16]{0:T(128)S(1)} %get-tuple-element.249, f32[1024,64]{0,1:T(8,128)S(1)} %get-tuple-element.223, f32[1024,64]{0,1:T(8,128)S(1)} %get-tuple-element.224), kind=kLoop, calls=%fused_computation.15.clone.1 | loop fusion | flops 14680064 | bytes 4980800 | tf_op jit(solution)/shard_map/while/body/eval_jaxpr/convert_element_type | solution.py:112
  364.3 17.0 %fusion.84 = (bf16[16,1024,64]{1,2,0:T(8,128)(2,1)S(1)}, bf16[16,1024,64]{1,2,0:T(8,128)(2,1)S(1)}) fusion(f32[1024,64]{0,1:T(8,128)S(1)} %get-tuple-element.248, f32[16]{0:T(128)S(1)} %get-tuple-element.249, f32[1024,64]{0,1:T(8,128)S(1)} %get-tuple-element.223, f32[1024,64]{0,1:T(8,128)S(1)} %get-tuple-element.224), kind=kLoop, calls=%fused_computation.15.clone.1 | loop fusion | flops 14680064 | bytes 4980800 | tf_op jit(solution)/shard_map/while/body/eval_jaxpr/convert_element_type | solution.py:112
  384.1 17.0 %fusion.84 = (bf16[16,1024,64]{1,2,0:T(8,128)(2,1)S(1)}, bf16[16,1024,64]{1,2,0:T(8,128)(2,1)S(1)}) fusion(f32[1024,64]{0,1:T(8,128)S(1)} %get-tuple-element.248, f32[16]{0:T(128)S(1)} %get-tuple-element.249, f32[1024,64]{0,1:T(8,128)S(1)} %get-tuple-element.223, f32[1024,64]{0,1:T(8,128)S(1)} %get-tuple-element.224), kind=kLoop, calls=%fused_computation.15.clone.1 | loop fusion | flops 14680064 | bytes 4980800 | tf_op jit(solution)/shard_map/while/body/eval_jaxpr/convert_element_type | solution.py:112
  404.0 17.0 %fusion.84 = (bf16[16,1024,64]{1,2,0:T(8,128)(2,1)S(1)}, bf16[16,1024,64]{1,2,0:T(8,128)(2,1)S(1)}) fusion(f32[1024,64]{0,1:T(8,128)S(1)} %get-tuple-element.248, f32[16]{0:T(128)S(1)} %get-tuple-element.249, f32[1024,64]{0,1:T(8,128)S(1)} %get-tuple-element.223, f32[1024,64]{0,1:T(8,128)S(1)} %get-tuple-element.224), kind=kLoop, calls=%fused_computation.15.clone.1 | loop fusion | flops 14680064 | bytes 4980800 | tf_op jit(solution)/shard_map/while/body/eval_jaxpr/convert_element_type | solution.py:112
  423.8 17.0 %fusion.84 = (bf16[16,1024,64]{1,2,0:T(8,128)(2,1)S(1)}, bf16[16,1024,64]{1,2,0:T(8,128)(2,1)S(1)}) fusion(f32[1024,64]{0,1:T(8,128)S(1)} %get-tuple-element.248, f32[16]{0:T(128)S(1)} %get-tuple-element.249, f32[1024,64]{0,1:T(8,128)S(1)} %get-tuple-element.223, f32[1024,64]{0,1:T(8,128)S(1)} %get-tuple-element.224), kind=kLoop, calls=%fused_computation.15.clone.1 | loop fusion | flops 14680064 | bytes 4980800 | tf_op jit(solution)/shard_map/while/body/eval_jaxpr/convert_element_type | solution.py:112
  443.7 17.0 %fusion.84 = (bf16[16,1024,64]{1,2,0:T(8,128)(2,1)S(1)}, bf16[16,1024,64]{1,2,0:T(8,128)(2,1)S(1)}) fusion(f32[1024,64]{0,1:T(8,128)S(1)} %get-tuple-element.248, f32[16]{0:T(128)S(1)} %get-tuple-element.249, f32[1024,64]{0,1:T(8,128)S(1)} %get-tuple-element.223, f32[1024,64]{0,1:T(8,128)S(1)} %get-tuple-element.224), kind=kLoop, calls=%fused_computation.15.clone.1 | loop fusion | flops 14680064 | bytes 4980800 | tf_op jit(solution)/shard_map/while/body/eval_jaxpr/convert_element_type | solution.py:112
  463.5 17.0 %fusion.84 = (bf16[16,1024,64]{1,2,0:T(8,128)(2,1)S(1)}, bf16[16,1024,64]{1,2,0:T(8,128)(2,1)S(1)}) fusion(f32[1024,64]{0,1:T(8,128)S(1)} %get-tuple-element.248, f32[16]{0:T(128)S(1)} %get-tuple-element.249, f32[1024,64]{0,1:T(8,128)S(1)} %get-tuple-element.223, f32[1024,64]{0,1:T(8,128)S(1)} %get-tuple-element.224), kind=kLoop, calls=%fused_computation.15.clone.1 | loop fusion | flops 14680064 | bytes 4980800 | tf_op jit(solution)/shard_map/while/body/eval_jaxpr/convert_element_type | solution.py:112
  483.4 17.0 %fusion.84 = (bf16[16,1024,64]{1,2,0:T(8,128)(2,1)S(1)}, bf16[16,1024,64]{1,2,0:T(8,128)(2,1)S(1)}) fusion(f32[1024,64]{0,1:T(8,128)S(1)} %get-tuple-element.248, f32[16]{0:T(128)S(1)} %get-tuple-element.249, f32[1024,64]{0,1:T(8,128)S(1)} %get-tuple-element.223, f32[1024,64]{0,1:T(8,128)S(1)} %get-tuple-element.224), kind=kLoop, calls=%fused_computation.15.clone.1 | loop fusion | flops 14680064 | bytes 4980800 | tf_op jit(solution)/shard_map/while/body/eval_jaxpr/convert_element_type | solution.py:112
  503.2 17.0 %fusion.84 = (bf16[16,1024,64]{1,2,0:T(8,128)(2,1)S(1)}, bf16[16,1024,64]{1,2,0:T(8,128)(2,1)S(1)}) fusion(f32[1024,64]{0,1:T(8,128)S(1)} %get-tuple-element.248, f32[16]{0:T(128)S(1)} %get-tuple-element.249, f32[1024,64]{0,1:T(8,128)S(1)} %get-tuple-element.223, f32[1024,64]{0,1:T(8,128)S(1)} %get-tuple-element.224), kind=kLoop, calls=%fused_computation.15.clone.1 | loop fusion | flops 14680064 | bytes 4980800 | tf_op jit(solution)/shard_map/while/body/eval_jaxpr/convert_element_type | solution.py:112
  523.0 17.0 %fusion.84 = (bf16[16,1024,64]{1,2,0:T(8,128)(2,1)S(1)}, bf16[16,1024,64]{1,2,0:T(8,128)(2,1)S(1)}) fusion(f32[1024,64]{0,1:T(8,128)S(1)} %get-tuple-element.248, f32[16]{0:T(128)S(1)} %get-tuple-element.249, f32[1024,64]{0,1:T(8,128)S(1)} %get-tuple-element.223, f32[1024,64]{0,1:T(8,128)S(1)} %get-tuple-element.224), kind=kLoop, calls=%fused_computation.15.clone.1 | loop fusion | flops 14680064 | bytes 4980800 | tf_op jit(solution)/shard_map/while/body/eval_jaxpr/convert_element_type | solution.py:112
  547.4 25.5 %all_to_all.33 = bf16[16,2,8192]{2,1,0:T(2,128)(2,1)S(1)} all-to-all(bf16[16,2,8192]{2,1,0:T(2,128)(2,1)S(1)} %reshape.331), channel_id=1, replica_groups=mesh['grp'=2,'chan'=16] {'chan'}, dimensions={0} | all-to-all | bytes 1048576 | tf_op jit(solution)/shard_map/all_to_all | solution.py:122
  (84 shorter events, 154.8 us)
Async XLA Ops:
  78.4 4.8 copy-start.1
  134.6 7.7 %copy-start = (f32[1024,64]{0,1:T(8,128)S(1)}, f32[1024,64]{0,1:T(8,128)}, u32[]{:S(2)}) copy-start(f32[1024,64]{0,1:T(8,128)} %param.7) | copy-start | bytes 786436
  134.7 48.8 %all-to-all-start = ((bf16[16,2,32768]{2,1,0:T(2,128)(2,1)}), bf16[16,2,32768]{2,1,0:T(2,128)(2,1)S(1)}, u32[]{:S(2)}, u32[]{:S(2)}) async-start(bf16[16,2,32768]{2,1,0:T(2,128)(2,1)} %reshape.329), calls=%async_computation | async-start | bytes 4194304 | tf_op jit(solution)/shard_map/all_to_all | solution.py:84
where the time goes:
time: 584 us; the launch traced here: 575 us
  other arithmetic  337 us (58%)
  local copies, waits for them, and re-layouts  116 us (20%)
  matrix products  62.9 us (11%)
  blocking collectives  25.5 us (4%)
  waiting for transfers between devices  24 us (4%)
  starting transfers between devices  7.66 us (1%)
    convert_element_type x16, other arithmetic, one_block(): w_real = (base_real * low_real - base_imag * low_imag).astype(jnp.bfloat16)  272 us
    unnamed x11, local copies, waits for them, and re-layouts  50.9 us
    dot_general x16, matrix products, one_block(): jnp.einsum('cnk,cbk->cnb', volt_part, weight_part, preferred_element_type...  27.9 us
    dot_general x1, matrix products, body(): jnp.einsum('irskm,qmj->irqsjk', twisted, table_three, precision=highest)  27.7 us
    all_to_all x1, blocking collectives, body(): lax.all_to_all(power_bins, 'chan', split_axis=1, concat_axis=2, tiled=True)  25.5 us
    all_to_all x1, waiting for transfers between devices, body(): lax.all_to_all(outgoing, 'chan', split_axis=0, concat_axis=3, tiled=True)  24 us
    mul x16, local copies, waits for them, and re-layouts, one_block(): w_real = (base_real * low_real - base_imag * low_imag).astype(jnp.bfloat16)  17.1 us
    mul x1, other arithmetic, rotation(): return (jnp.cos(angle) * scale, -jnp.sin(angle) * scale)  17 us
  transfers between devices with their start and end apart: 1, of which 1 were waited for; matrix products, arithmetic and copies ran while one was open for 3% of the time, Pallas kernels for 0%

commit v1 on v0

--- a/solution.py
+++ b/solution.py
@@ -81,7 +81,19 @@
     volt_real = (spec_real * gain_row).astype(jnp.bfloat16)
     volt_imag = (spec_imag * gain_row).astype(jnp.bfloat16)
     outgoing = jnp.stack([volt_real, volt_imag], axis=1).transpose(3, 1, 2, 0)
-    arrived = lax.all_to_all(outgoing, "chan", split_axis=0, concat_axis=3, tiled=True)
+    ways, here = (lax.axis_size("chan"), lax.axis_index("chan"))
+    width = outgoing.shape[0] // ways
+    shape = list(outgoing.shape)
+    shape[0] = width
+    height = shape[3]
+    shape[3] = height * ways
+    full = jnp.zeros(shape, outgoing.dtype)
+    for mask in range(ways):
+        part = lax.dynamic_slice_in_dim(outgoing, (here ^ mask) * width, width, axis=0)
+        if mask:
+            part = lax.ppermute(part, "chan", [(d, d ^ mask) for d in range(ways)])
+        full = lax.dynamic_update_slice_in_dim(full, part, (here ^ mask) * height, axis=3)
+    arrived = full
     dish_volts = arrived.reshape(chan_here, 2, SPEC, DISHES, POLS).transpose(0, 1, 4, 2, 3)
     real_part = dish_volts[:, 0]
     imag_part = dish_volts[:, 1]

time: 584 us -> 531 us (0.909)
  local copies, waits for them, and re-layouts: 116 us -> 57.2 us
  starting transfers between devices: 7.66 us -> 20 us
    unnamed x11 -> x12, local copies, waits for them, and re-layouts: 50.9 us -> 3 us
    all_to_all x1 -> x0, waiting for transfers between devices: 24 us -> none  [body(): lax.all_to_all(outgoing, 'chan', split_axis=0, concat_axis=3, tiled=True)]
    ppermute x0 -> x15, starting transfers between devices: none -> 20 us  [body(): part = lax.ppermute(part, 'chan', [(d, d ^ mask) for d in range(ways)])]
    ppermute x0 -> x15, waiting for transfers between devices: none -> 18.7 us  [body(): part = lax.ppermute(part, 'chan', [(d, d ^ mask) for d in range(ways)])]
    dynamic_update_slice x0 -> x15, local copies, waits for them, and re-layouts: none -> 14.6 us  [body(): lax.dynamic_update_slice_in_dim(full, part, (here ^ mask) * height, axis=3)]
    all_to_all x1 -> x0, local copies, waits for them, and re-layouts: 14.6 us -> none  [body(): lax.all_to_all(outgoing, 'chan', split_axis=0, concat_axis=3, tiled=True)]
    another operation x1 -> x0, local copies, waits for them, and re-layouts: 14 us -> none  [body(): outgoing = jnp.stack([volt_real, volt_imag], axis=1).transpose(3, 1, 2, 0)]
    all_to_all x1 -> x0, starting transfers between devices: 7.66 us -> none  [body(): lax.all_to_all(outgoing, 'chan', split_axis=0, concat_axis=3, tiled=True)]
  transfers between devices with their start and end apart: 1 -> 15, of which waited for: 1 -> 4; matrix products, arithmetic and copies ran while one was open for 3% -> 6% of each run, Pallas kernels for 0% -> 0%
where the time goes in v1:
time: 531 us; the launch traced here: 523 us
  other arithmetic  339 us (64%)
  matrix products  62.9 us (12%)
  local copies, waits for them, and re-layouts  57.2 us (11%)
  blocking collectives  23 us (4%)
  starting transfers between devices  20 us (4%)
  waiting for transfers between devices  18.7 us (4%)
    convert_element_type x16, other arithmetic, one_block(): w_real = (base_real * low_real - base_imag * low_imag).astype(jnp.bfloat16)  272 us
    dot_general x16, matrix products, one_block(): jnp.einsum('cnk,cbk->cnb', volt_part, weight_part, preferred_element_type...  28 us
    dot_general x1, matrix products, body(): jnp.einsum('irskm,qmj->irqsjk', twisted, table_three, precision=highest)  27.7 us
    all_to_all x1, blocking collectives, body(): lax.all_to_all(power_bins, 'chan', split_axis=1, concat_axis=2, tiled=True)  23 us
    ppermute x15, starting transfers between devices, body(): part = lax.ppermute(part, 'chan', [(d, d ^ mask) for d in range(ways)])  20 us
    ppermute x15, waiting for transfers between devices, body(): part = lax.ppermute(part, 'chan', [(d, d ^ mask) for d in range(ways)])  18.7 us
    mul x1, other arithmetic, rotation(): return (jnp.cos(angle) * scale, -jnp.sin(angle) * scale)  17.2 us
    mul x16, local copies, waits for them, and re-layouts, one_block(): w_real = (base_real * low_real - base_imag * low_imag).astype(jnp.bfloat16)  17.1 us
  transfers between devices with their start and end apart: 15, of which 4 were waited for; matrix products, arithmetic and copies ran while one was open for 6% of the time, Pallas kernels for 0%

profile of v1, /device:TPU:0, one launch (start us, length us, event | category | flops | bytes accessed | tf_op | source)
XLA Modules:
  0.0 522.7 jit_solution(8344614127759193988)
XLA Ops:
  9.0 16.8 %add_bitcast_fusion = f32[8,16,64,128,1]{3,0,2,1,4:T(8,128)S(1)} fusion(bf16[8,31,8192]{2,0,1:T(8,128)(2,1)} %param.5, f32[8192]{0:T(1024)S(1)} %get-tuple-element.159, f32[8192]{0:T(1024)S(1)} %get-tuple-element.160, f32[8192]{0:T(1024)S(1)} %get-tuple-element.161, f32[8192]{0:T(1024)S(1)} %get-tuple-element.162, f32[8192]{0:T(1024)S(1)} %get-tuple-element.163, ...), kind=kLoop, calls=%fused_computation.74 | loop fusion | flops 49283072 | bytes 38273024 | tf_op jit(solution)/shard_map/reshape | solution.py:65
  35.1 27.7 %fusion.27 = f32[8,2,2,16,64,64]{5,4,3,1,0,2:T(8,128)} fusion(f32[1,128,64]{1,2,0:T(8,128)S(1)} %get-tuple-element.182, f32[1,128,64]{1,2,0:T(8,128)S(1)} %get-tuple-element.183, f32[8,1,16,64,128]{4,3,1,2,0:T(8,128)S(1)} %get-tuple-element.138, f32[8,1,16,64,128]{4,3,1,2,0:T(8,128)S(1)} %get-tuple-element.137), kind=kOutput, calls=%fused_computation.30 | convolution fusion | flops 3223339008 | bytes 16842752 | tf_op jit(solution)/shard_map/irskm,qmj->irqsjk/dot_general | solution.py:73
  62.8 12.1 %slice_subtract_fusion = (f32[8,1,1,16,64,64]{5,4,3,1,0,2:T(8,128)}, f32[8,1,1,16,64,64]{5,4,3,1,0,2:T(8,128)}) fusion(f32[8,2,2,16,64,64]{5,4,3,1,0,2:T(8,128)} %fusion.27), kind=kLoop, calls=%fused_computation.66 | loop fusion | flops 1048576 | bytes 12582912 | tf_op jit(solution)/shard_map/sub | solution.py:74
  96.6 17.2 %negate_multiply_fusion = (f32[16,1024,64]{1,2,0:T(8,128)}, f32[16,1024,64]{1,2,0:T(8,128)}) fusion(f32[1024,64]{0,1:T(8,128)S(1)} %copy-done.2, f32[16]{0:T(128)S(1)} %add_convert_fusion), kind=kLoop, calls=%fused_computation.70 | loop fusion | flops 8388608 | bytes 8650816 | tf_op jit(solution)/shard_map/mul | solution.py:115
  133.4 8.4 %collective-permute-done.7 = bf16[256,2,16,8]{0,2,3,1:T(8,128)(2,1)S(1)} collective-permute-done((bf16[256,2,16,8]{0,2,3,1:T(8,128)(2,1)S(1)}, bf16[256,2,16,8]{0,2,3,1:T(8,128)(2,1)S(1)}, u32[]{:S(2)}, u32[]{:S(2)}) %collective-permute-start.7) | collective-permute-done | bytes 131104 | tf_op jit(solution)/shard_map/ppermute | solution.py:94
  165.8 9.0 %copy.34 = bf16[256,2,2,16,128]{4,3,2,1,0:T(8,128)(2,1)} copy(bf16[256,2,2,16,128]{0,3,2,4,1:T(8,128)(2,1)} %pad_maximum_fusion.1) | data formatting | bytes 8388608 | tf_op jit(solution)/shard_map/stack | solution.py:100
  174.9 317.5 %while.12 = (s32[]{:T(128)}, bf16[16,16,1,1024]{3,1,0,2:T(8,128)(2,1)S(1)}, bf16[16,16,64,128]{3,2,1,0:T(8,128)(2,1)}, f32[16,1024,64]{1,2,0:T(8,128)}, f32[16,1...) while((s32[]{:T(128)}, ...), condition=%wide.region_3.4_spmd.clone.clone, body=%wide.region_1.3_spmd.clone.clone.sunk | while | flops 293601280 | bytes 10683037 | solution.py:132
  175.9 17.0 %fusion.113 = (bf16[16,1024,64]{1,2,0:T(8,128)(2,1)S(1)}, bf16[16,1024,64]{1,2,0:T(8,128)(2,1)S(1)}) fusion(f32[1024,64]{0,1:T(8,128)S(1)} %get-tuple-element.256, f32[16]{0:T(128)S(1)} %get-tuple-element.257, f32[1024,64]{0,1:T(8,128)S(1)} %get-tuple-element.231, f32[1024,64]{0,1:T(8,128)S(1)} %get-tuple-element.232), kind=kLoop, calls=%fused_computation.15.clone.1 | loop fusion | flops 14680064 | bytes 4980800 | tf_op jit(solution)/shard_map/while/body/eval_jaxpr/convert_element_type | solution.py:124
  195.8 17.0 %fusion.113 = (bf16[16,1024,64]{1,2,0:T(8,128)(2,1)S(1)}, bf16[16,1024,64]{1,2,0:T(8,128)(2,1)S(1)}) fusion(f32[1024,64]{0,1:T(8,128)S(1)} %get-tuple-element.256, f32[16]{0:T(128)S(1)} %get-tuple-element.257, f32[1024,64]{0,1:T(8,128)S(1)} %get-tuple-element.231, f32[1024,64]{0,1:T(8,128)S(1)} %get-tuple-element.232), kind=kLoop, calls=%fused_computation.15.clone.1 | loop fusion | flops 14680064 | bytes 4980800 | tf_op jit(solution)/shard_map/while/body/eval_jaxpr/convert_element_type | solution.py:124
  215.6 17.0 %fusion.113 = (bf16[16,1024,64]{1,2,0:T(8,128)(2,1)S(1)}, bf16[16,1024,64]{1,2,0:T(8,128)(2,1)S(1)}) fusion(f32[1024,64]{0,1:T(8,128)S(1)} %get-tuple-element.256, f32[16]{0:T(128)S(1)} %get-tuple-element.257, f32[1024,64]{0,1:T(8,128)S(1)} %get-tuple-element.231, f32[1024,64]{0,1:T(8,128)S(1)} %get-tuple-element.232), kind=kLoop, calls=%fused_computation.15.clone.1 | loop fusion | flops 14680064 | bytes 4980800 | tf_op jit(solution)/shard_map/while/body/eval_jaxpr/convert_element_type | solution.py:124
  235.5 17.0 %fusion.113 = (bf16[16,1024,64]{1,2,0:T(8,128)(2,1)S(1)}, bf16[16,1024,64]{1,2,0:T(8,128)(2,1)S(1)}) fusion(f32[1024,64]{0,1:T(8,128)S(1)} %get-tuple-element.256, f32[16]{0:T(128)S(1)} %get-tuple-element.257, f32[1024,64]{0,1:T(8,128)S(1)} %get-tuple-element.231, f32[1024,64]{0,1:T(8,128)S(1)} %get-tuple-element.232), kind=kLoop, calls=%fused_computation.15.clone.1 | loop fusion | flops 14680064 | bytes 4980800 | tf_op jit(solution)/shard_map/while/body/eval_jaxpr/convert_element_type | solution.py:124
  255.3 17.0 %fusion.113 = (bf16[16,1024,64]{1,2,0:T(8,128)(2,1)S(1)}, bf16[16,1024,64]{1,2,0:T(8,128)(2,1)S(1)}) fusion(f32[1024,64]{0,1:T(8,128)S(1)} %get-tuple-element.256, f32[16]{0:T(128)S(1)} %get-tuple-element.257, f32[1024,64]{0,1:T(8,128)S(1)} %get-tuple-element.231, f32[1024,64]{0,1:T(8,128)S(1)} %get-tuple-element.232), kind=kLoop, calls=%fused_computation.15.clone.1 | loop fusion | flops 14680064 | bytes 4980800 | tf_op jit(solution)/shard_map/while/body/eval_jaxpr/convert_element_type | solution.py:124
  275.1 17.0 %fusion.113 = (bf16[16,1024,64]{1,2,0:T(8,128)(2,1)S(1)}, bf16[16,1024,64]{1,2,0:T(8,128)(2,1)S(1)}) fusion(f32[1024,64]{0,1:T(8,128)S(1)} %get-tuple-element.256, f32[16]{0:T(128)S(1)} %get-tuple-element.257, f32[1024,64]{0,1:T(8,128)S(1)} %get-tuple-element.231, f32[1024,64]{0,1:T(8,128)S(1)} %get-tuple-element.232), kind=kLoop, calls=%fused_computation.15.clone.1 | loop fusion | flops 14680064 | bytes 4980800 | tf_op jit(solution)/shard_map/while/body/eval_jaxpr/convert_element_type | solution.py:124
  295.0 17.0 %fusion.113 = (bf16[16,1024,64]{1,2,0:T(8,128)(2,1)S(1)}, bf16[16,1024,64]{1,2,0:T(8,128)(2,1)S(1)}) fusion(f32[1024,64]{0,1:T(8,128)S(1)} %get-tuple-element.256, f32[16]{0:T(128)S(1)} %get-tuple-element.257, f32[1024,64]{0,1:T(8,128)S(1)} %get-tuple-element.231, f32[1024,64]{0,1:T(8,128)S(1)} %get-tuple-element.232), kind=kLoop, calls=%fused_computation.15.clone.1 | loop fusion | flops 14680064 | bytes 4980800 | tf_op jit(solution)/shard_map/while/body/eval_jaxpr/convert_element_type | solution.py:124
  314.8 17.0 %fusion.113 = (bf16[16,1024,64]{1,2,0:T(8,128)(2,1)S(1)}, bf16[16,1024,64]{1,2,0:T(8,128)(2,1)S(1)}) fusion(f32[1024,64]{0,1:T(8,128)S(1)} %get-tuple-element.256, f32[16]{0:T(128)S(1)} %get-tuple-element.257, f32[1024,64]{0,1:T(8,128)S(1)} %get-tuple-element.231, f32[1024,64]{0,1:T(8,128)S(1)} %get-tuple-element.232), kind=kLoop, calls=%fused_computation.15.clone.1 | loop fusion | flops 14680064 | bytes 4980800 | tf_op jit(solution)/shard_map/while/body/eval_jaxpr/convert_element_type | solution.py:124
  334.7 17.0 %fusion.113 = (bf16[16,1024,64]{1,2,0:T(8,128)(2,1)S(1)}, bf16[16,1024,64]{1,2,0:T(8,128)(2,1)S(1)}) fusion(f32[1024,64]{0,1:T(8,128)S(1)} %get-tuple-element.256, f32[16]{0:T(128)S(1)} %get-tuple-element.257, f32[1024,64]{0,1:T(8,128)S(1)} %get-tuple-element.231, f32[1024,64]{0,1:T(8,128)S(1)} %get-tuple-element.232), kind=kLoop, calls=%fused_computation.15.clone.1 | loop fusion | flops 14680064 | bytes 4980800 | tf_op jit(solution)/shard_map/while/body/eval_jaxpr/convert_element_type | solution.py:124
  354.5 17.0 %fusion.113 = (bf16[16,1024,64]{1,2,0:T(8,128)(2,1)S(1)}, bf16[16,1024,64]{1,2,0:T(8,128)(2,1)S(1)}) fusion(f32[1024,64]{0,1:T(8,128)S(1)} %get-tuple-element.256, f32[16]{0:T(128)S(1)} %get-tuple-element.257, f32[1024,64]{0,1:T(8,128)S(1)} %get-tuple-element.231, f32[1024,64]{0,1:T(8,128)S(1)} %get-tuple-element.232), kind=kLoop, calls=%fused_computation.15.clone.1 | loop fusion | flops 14680064 | bytes 4980800 | tf_op jit(solution)/shard_map/while/body/eval_jaxpr/convert_element_type | solution.py:124
  374.4 17.0 %fusion.113 = (bf16[16,1024,64]{1,2,0:T(8,128)(2,1)S(1)}, bf16[16,1024,64]{1,2,0:T(8,128)(2,1)S(1)}) fusion(f32[1024,64]{0,1:T(8,128)S(1)} %get-tuple-element.256, f32[16]{0:T(128)S(1)} %get-tuple-element.257, f32[1024,64]{0,1:T(8,128)S(1)} %get-tuple-element.231, f32[1024,64]{0,1:T(8,128)S(1)} %get-tuple-element.232), kind=kLoop, calls=%fused_computation.15.clone.1 | loop fusion | flops 14680064 | bytes 4980800 | tf_op jit(solution)/shard_map/while/body/eval_jaxpr/convert_element_type | solution.py:124
  394.2 17.0 %fusion.113 = (bf16[16,1024,64]{1,2,0:T(8,128)(2,1)S(1)}, bf16[16,1024,64]{1,2,0:T(8,128)(2,1)S(1)}) fusion(f32[1024,64]{0,1:T(8,128)S(1)} %get-tuple-element.256, f32[16]{0:T(128)S(1)} %get-tuple-element.257, f32[1024,64]{0,1:T(8,128)S(1)} %get-tuple-element.231, f32[1024,64]{0,1:T(8,128)S(1)} %get-tuple-element.232), kind=kLoop, calls=%fused_computation.15.clone.1 | loop fusion | flops 14680064 | bytes 4980800 | tf_op jit(solution)/shard_map/while/body/eval_jaxpr/convert_element_type | solution.py:124
  414.1 17.0 %fusion.113 = (bf16[16,1024,64]{1,2,0:T(8,128)(2,1)S(1)}, bf16[16,1024,64]{1,2,0:T(8,128)(2,1)S(1)}) fusion(f32[1024,64]{0,1:T(8,128)S(1)} %get-tuple-element.256, f32[16]{0:T(128)S(1)} %get-tuple-element.257, f32[1024,64]{0,1:T(8,128)S(1)} %get-tuple-element.231, f32[1024,64]{0,1:T(8,128)S(1)} %get-tuple-element.232), kind=kLoop, calls=%fused_computation.15.clone.1 | loop fusion | flops 14680064 | bytes 4980800 | tf_op jit(solution)/shard_map/while/body/eval_jaxpr/convert_element_type | solution.py:124
  433.9 17.0 %fusion.113 = (bf16[16,1024,64]{1,2,0:T(8,128)(2,1)S(1)}, bf16[16,1024,64]{1,2,0:T(8,128)(2,1)S(1)}) fusion(f32[1024,64]{0,1:T(8,128)S(1)} %get-tuple-element.256, f32[16]{0:T(128)S(1)} %get-tuple-element.257, f32[1024,64]{0,1:T(8,128)S(1)} %get-tuple-element.231, f32[1024,64]{0,1:T(8,128)S(1)} %get-tuple-element.232), kind=kLoop, calls=%fused_computation.15.clone.1 | loop fusion | flops 14680064 | bytes 4980800 | tf_op jit(solution)/shard_map/while/body/eval_jaxpr/convert_element_type | solution.py:124
  453.7 17.0 %fusion.113 = (bf16[16,1024,64]{1,2,0:T(8,128)(2,1)S(1)}, bf16[16,1024,64]{1,2,0:T(8,128)(2,1)S(1)}) fusion(f32[1024,64]{0,1:T(8,128)S(1)} %get-tuple-element.256, f32[16]{0:T(128)S(1)} %get-tuple-element.257, f32[1024,64]{0,1:T(8,128)S(1)} %get-tuple-element.231, f32[1024,64]{0,1:T(8,128)S(1)} %get-tuple-element.232), kind=kLoop, calls=%fused_computation.15.clone.1 | loop fusion | flops 14680064 | bytes 4980800 | tf_op jit(solution)/shard_map/while/body/eval_jaxpr/convert_element_type | solution.py:124
  473.6 17.0 %fusion.113 = (bf16[16,1024,64]{1,2,0:T(8,128)(2,1)S(1)}, bf16[16,1024,64]{1,2,0:T(8,128)(2,1)S(1)}) fusion(f32[1024,64]{0,1:T(8,128)S(1)} %get-tuple-element.256, f32[16]{0:T(128)S(1)} %get-tuple-element.257, f32[1024,64]{0,1:T(8,128)S(1)} %get-tuple-element.231, f32[1024,64]{0,1:T(8,128)S(1)} %get-tuple-element.232), kind=kLoop, calls=%fused_computation.15.clone.1 | loop fusion | flops 14680064 | bytes 4980800 | tf_op jit(solution)/shard_map/while/body/eval_jaxpr/convert_element_type | solution.py:124
  497.9 23.0 %all_to_all.18 = bf16[16,2,8192]{2,1,0:T(2,128)(2,1)S(1)} all-to-all(bf16[16,2,8192]{2,1,0:T(2,128)(2,1)S(1)} %reshape.328), channel_id=1, replica_groups=mesh['grp'=2,'chan'=16] {'chan'}, dimensions={0} | all-to-all | bytes 1048576 | tf_op jit(solution)/shard_map/all_to_all | solution.py:134
  (130 shorter events, 134.9 us)
Async XLA Ops:
  79.7 4.8 copy-start.3
  87.1 9.6 %copy-start.2 = (f32[1024,64]{0,1:T(8,128)S(1)}, f32[1024,64]{0,1:T(8,128)}, u32[]{:S(2)}) copy-start(f32[1024,64]{0,1:T(8,128)} %param.7) | copy-start | bytes 786436
  87.1 67.6 %collective-permute-start.10 = (bf16[256,2,16,8]{0,2,3,1:T(8,128)(2,1)S(1)}, bf16[256,2,16,8]{0,2,3,1:T(8,128)(2,1)}, u32[]{:S(2)}, u32[]{:S(2)}) collective-permute-start(bf16[256,2,16,8]{0,2,3,1:T(8,128)(2,1)S(1)} %get-tuple-element.154), channel_id=1, source_target_pairs={{0,11},{1,10},{2,9},{3,8},{4,15},{5,14},{6,13},{7,12},{8,3},{9,2},... | collective-permute-start | bytes 393224 | tf_op jit(solution)/shard_map/ppermute | solution.py:94
  92.3 35.0 %collective-permute-start.5 = (bf16[256,2,16,8]{0,2,3,1:T(8,128)(2,1)}, bf16[256,2,16,8]{0,2,3,1:T(8,128)(2,1)}, u32[]{:S(2)}, u32[]{:S(2)}) collective-permute-start(bf16[256,2,16,8]{0,2,3,1:T(8,128)(2,1)} %get-tuple-element.148), channel_id=1, source_target_pairs={{0,6},{1,7},{2,4},{3,5},{4,2},{5,3},{6,0},{7,1},{8,14},{9,15},{10,... | collective-permute-start | bytes 393224 | tf_op jit(solution)/shard_map/ppermute | solution.py:94
  94.7 20.8 %collective-permute-start = (bf16[256,2,16,8]{0,2,3,1:T(8,128)(2,1)}, bf16[256,2,16,8]{0,2,3,1:T(8,128)(2,1)}, u32[]{:S(2)}, u32[]{:S(2)}) collective-permute-start(bf16[256,2,16,8]{0,2,3,1:T(8,128)(2,1)} %get-tuple-element.142), channel_id=1, source_target_pairs={{0,1},{1,0},{2,3},{3,2},{4,5},{5,4},{6,7},{7,6},{8,9},{9,8},{10,11... | collective-permute-start | bytes 393224 | tf_op jit(solution)/shard_map/ppermute | solution.py:94
  95.1 22.4 %collective-permute-start.1 = (bf16[256,2,16,8]{0,2,3,1:T(8,128)(2,1)}, bf16[256,2,16,8]{0,2,3,1:T(8,128)(2,1)}, u32[]{:S(2)}, u32[]{:S(2)}) collective-permute-start(bf16[256,2,16,8]{0,2,3,1:T(8,128)(2,1)} %get-tuple-element.143), channel_id=1, source_target_pairs={{0,2},{1,3},{2,0},{3,1},{4,6},{5,7},{6,4},{7,5},{8,10},{9,11},{10,... | collective-permute-start | bytes 393224 | tf_op jit(solution)/shard_map/ppermute | solution.py:94
  96.6 24.0 %collective-permute-start.2 = (bf16[256,2,16,8]{0,2,3,1:T(8,128)(2,1)}, bf16[256,2,16,8]{0,2,3,1:T(8,128)(2,1)}, u32[]{:S(2)}, u32[]{:S(2)}) collective-permute-start(bf16[256,2,16,8]{0,2,3,1:T(8,128)(2,1)} %get-tuple-element.144), channel_id=1, source_target_pairs={{0,3},{1,2},{2,1},{3,0},{4,7},{5,6},{6,5},{7,4},{8,11},{9,10},{10,... | collective-permute-start | bytes 393224 | tf_op jit(solution)/shard_map/ppermute | solution.py:94
  114.0 1.4 copy-start
  115.4 7.8 %collective-permute-start.3 = (bf16[256,2,16,8]{0,2,3,1:T(8,128)(2,1)}, bf16[256,2,16,8]{0,2,3,1:T(8,128)(2,1)S(1)}, u32[]{:S(2)}, u32[]{:S(2)}) collective-permute-start(bf16[256,2,16,8]{0,2,3,1:T(8,128)(2,1)} %get-tuple-element.145), channel_id=1, source_target_pairs={{0,4},{1,5},{2,6},{3,7},{4,0},{5,1},{6,2},{7,3},{8,12},{9,13},{10,... | collective-permute-start | bytes 393224 | tf_op jit(solution)/shard_map/ppermute | solution.py:94
  117.5 6.9 %collective-permute-start.4 = (bf16[256,2,16,8]{0,2,3,1:T(8,128)(2,1)}, bf16[256,2,16,8]{0,2,3,1:T(8,128)(2,1)S(1)}, u32[]{:S(2)}, u32[]{:S(2)}) collective-permute-start(bf16[256,2,16,8]{0,2,3,1:T(8,128)(2,1)} %get-tuple-element.146), channel_id=1, source_target_pairs={{0,5},{1,4},{2,7},{3,6},{4,1},{5,0},{6,3},{7,2},{8,13},{9,12},{10,... | collective-permute-start | bytes 393224 | tf_op jit(solution)/shard_map/ppermute | solution.py:94
  120.6 10.0 %collective-permute-start.6 = (bf16[256,2,16,8]{0,2,3,1:T(8,128)(2,1)S(1)}, bf16[256,2,16,8]{0,2,3,1:T(8,128)(2,1)S(1)}, u32[]{:S(2)}, u32[]{:S(2)}) collective-permute-start(bf16[256,2,16,8]{0,2,3,1:T(8,128)(2,1)S(1)} %get-tuple-element.149), channel_id=1, source_target_pairs={{0,7},{1,6},{2,5},{3,4},{4,3},{5,2},{6,1},{7,0},{8,15},{9,14},{10,... | collective-permute-start | bytes 393224 | tf_op jit(solution)/shard_map/ppermute | solution.py:94
  123.3 18.5 %collective-permute-start.7 = (bf16[256,2,16,8]{0,2,3,1:T(8,128)(2,1)S(1)}, bf16[256,2,16,8]{0,2,3,1:T(8,128)(2,1)S(1)}, u32[]{:S(2)}, u32[]{:S(2)}) collective-permute-start(bf16[256,2,16,8]{0,2,3,1:T(8,128)(2,1)S(1)} %get-tuple-element.150), channel_id=1, source_target_pairs={{0,8},{1,9},{2,10},{3,11},{4,12},{5,13},{6,14},{7,15},{8,0},{9,1},... | collective-permute-start | bytes 393224 | tf_op jit(solution)/shard_map/ppermute | solution.py:94
  124.4 19.2 %collective-permute-start.8 = (bf16[256,2,16,8]{0,2,3,1:T(8,128)(2,1)S(1)}, bf16[256,2,16,8]{0,2,3,1:T(8,128)(2,1)S(1)}, u32[]{:S(2)}, u32[]{:S(2)}) collective-permute-start(bf16[256,2,16,8]{0,2,3,1:T(8,128)(2,1)S(1)} %get-tuple-element.151), channel_id=1, source_target_pairs={{0,9},{1,8},{2,11},{3,10},{4,13},{5,12},{6,15},{7,14},{8,1},{9,0},... | collective-permute-start | bytes 393224 | tf_op jit(solution)/shard_map/ppermute | solution.py:94
  127.3 25.7 %collective-permute-start.9 = (bf16[256,2,16,8]{0,2,3,1:T(8,128)(2,1)S(1)}, bf16[256,2,16,8]{0,2,3,1:T(8,128)(2,1)S(1)}, u32[]{:S(2)}, u32[]{:S(2)}) collective-permute-start(bf16[256,2,16,8]{0,2,3,1:T(8,128)(2,1)S(1)} %get-tuple-element.152), channel_id=1, source_target_pairs={{0,10},{1,11},{2,8},{3,9},{4,14},{5,15},{6,12},{7,13},{8,2},{9,3},... | collective-permute-start | bytes 393224 | tf_op jit(solution)/shard_map/ppermute | solution.py:94
  130.6 25.7 %collective-permute-start.11 = (bf16[256,2,16,8]{0,2,3,1:T(8,128)(2,1)S(1)}, bf16[256,2,16,8]{0,2,3,1:T(8,128)(2,1)S(1)}, u32[]{:S(2)}, u32[]{:S(2)}) collective-permute-start(bf16[256,2,16,8]{0,2,3,1:T(8,128)(2,1)S(1)} %get-tuple-element.155), channel_id=1, source_target_pairs={{0,12},{1,13},{2,14},{3,15},{4,8},{5,9},{6,10},{7,11},{8,4},{9,5},... | collective-permute-start | bytes 393224 | tf_op jit(solution)/shard_map/ppermute | solution.py:94
  141.8 15.2 %collective-permute-start.12 = (bf16[256,2,16,8]{0,2,3,1:T(8,128)(2,1)S(1)}, bf16[256,2,16,8]{0,2,3,1:T(8,128)(2,1)S(1)}, u32[]{:S(2)}, u32[]{:S(2)}) collective-permute-start(bf16[256,2,16,8]{0,2,3,1:T(8,128)(2,1)S(1)} %get-tuple-element.153), channel_id=1, source_target_pairs={{0,13},{1,12},{2,15},{3,14},{4,9},{5,8},{6,11},{7,10},{8,5},{9,4},... | collective-permute-start | bytes 393224 | tf_op jit(solution)/shard_map/ppermute | solution.py:94
  143.6 14.1 %collective-permute-start.13 = (bf16[256,2,16,8]{0,2,3,1:T(8,128)(2,1)S(1)}, bf16[256,2,16,8]{0,2,3,1:T(8,128)(2,1)S(1)}, u32[]{:S(2)}, u32[]{:S(2)}) collective-permute-start(bf16[256,2,16,8]{0,2,3,1:T(8,128)(2,1)S(1)} %get-tuple-element.147), channel_id=1, source_target_pairs={{0,14},{1,15},{2,12},{3,13},{4,10},{5,11},{6,8},{7,9},{8,6},{9,7},... | collective-permute-start | bytes 393224 | tf_op jit(solution)/shard_map/ppermute | solution.py:94
  153.0 7.2 %collective-permute-start.14 = (bf16[256,2,16,8]{0,2,3,1:T(8,128)(2,1)S(1)}, bf16[256,2,16,8]{0,2,3,1:T(8,128)(2,1)S(1)}, u32[]{:S(2)}, u32[]{:S(2)}) collective-permute-start(bf16[256,2,16,8]{0,2,3,1:T(8,128)(2,1)S(1)} %get-tuple-element.141), channel_id=1, source_target_pairs={{0,15},{1,14},{2,13},{3,12},{4,11},{5,10},{6,9},{7,8},{8,7},{9,6},... | collective-permute-start | bytes 393224 | tf_op jit(solution)/shard_map/ppermute | solution.py:94
  160.8 2.2 copy-start.1
